TPU v7x, 512 devices: a whole 4x4x16 slice. The times are simulated.
512 devices in a mesh: grp: 16 (over z), lat: 32 (over y, x, core).
Axes of the slice: x: 4, y: 4, z: 16, core: 2. Of those that a mesh axis runs over, the one named last changes fastest.
Arguments:
- stream: bfloat16 [256, 8192], P('lat'), may hold values from -26 to 26
- batch_index: int32 [256], replicated, may hold values from 0 to 255
- weight: bfloat16 [8192, 65536], P(None, ('grp', 'lat')), may hold values from -0.26516504 to 0.26516504
- enc_bias: float32 [65536], P(('grp', 'lat')), may hold values from -1.5 to 0.5
- dec_bias: float32 [8192], replicated, may hold values from -3 to 3
Outputs:
- weight_grad: bfloat16 [8192, 65536], P(None, ('grp', 'lat'))
- bias_grad: float32 [65536], P(('grp', 'lat'))
- recon_error: bfloat16 [256, 8192], P('lat')
All inputs are finite; a program needn't handle non-finite values.
Results may differ from a plain program's by a relative error of at most 0.025.
Values may be sent and summed in bfloat16 or wider, within the bound.
No kernel may reach another device: no remote copies, remote signals or barrier semaphores. Data moves between devices by JAX's collectives and lax.ppermute only.
A program may use at most 64 MiB of HBM per device.

v0:
```python
import jax
import jax.numpy as jnp
import numpy as np
from jax import lax
from jax.sharding import Mesh
from jax.sharding import PartitionSpec as P

sharpness = 8.0
penalty = 0.25
epsilon = 1e-06
LAT = ("chip", "core")
ALL = ("grp", "chip", "core")


def xor_pairs(n, bit):
    return [(i, i ^ 1 << bit) for i in range(n)]


def butterfly_sum(x, axis, n, send_dtype):
    acc = x
    for bit in range(n.bit_length() - 1):
        sent = acc.astype(send_dtype)
        acc = sent.astype(jnp.float32) + lax.ppermute(sent, axis, xor_pairs(n, bit)).astype(
            jnp.float32
        )
    return acc


def swap_cores(x):
    return lax.ppermute(x, "core", [(0, 1), (1, 0)])


def body(stream, batch_index, weight, enc_bias, dec_bias):
    own_rows = stream.shape[0]
    n_chip = lax.axis_size("chip")
    n_grp = lax.axis_size("grp")
    chip = lax.axis_index("chip")
    core = lax.axis_index("core")
    half = n_chip * own_rows
    n_tok = batch_index.shape[0]
    mine = lax.all_gather(stream, "chip", axis=0, tiled=True)
    gathered = jnp.concatenate([mine, swap_cores(mine)], axis=0)
    q = jnp.arange(n_tok, dtype=jnp.int32)
    side = q // half
    q_chip = q % half // own_rows
    q_row = q % own_rows
    q_core = jnp.where(side == 0, core, 1 - core)
    token = (q_chip * 2 + q_core) * own_rows + q_row
    src = jnp.take(batch_index, token)
    s_chip = src // (2 * own_rows)
    s_core = src // own_rows % 2
    place = jnp.where(s_core == core, 0, half) + s_chip * own_rows + src % own_rows
    onehot = (
        place[:, None] == lax.broadcasted_iota(jnp.int32, (n_tok, gathered.shape[0]), 1)
    ).astype(gathered.dtype)
    batch = jnp.dot(onehot, gathered, preferred_element_type=jnp.float32).astype(jnp.bfloat16)
    centered = (batch.astype(jnp.float32) - dec_bias).astype(jnp.bfloat16)
    preact = jnp.dot(centered, weight, preferred_element_type=jnp.float32) + enc_bias
    active = (jax.nn.softplus(sharpness * preact) / sharpness).astype(jnp.bfloat16)
    own_batch = lax.dynamic_slice_in_dim(batch, chip * own_rows, own_rows, 0)
    partial = lax.dot_general(
        active, weight, (((1,), (1,)), ((), ())), preferred_element_type=jnp.float32
    ).astype(jnp.bfloat16)
    halves = partial.reshape(2, n_chip, own_rows, partial.shape[1])
    by_core = jnp.where(core == 0, halves, halves[::-1])
    lat_order = jnp.swapaxes(by_core, 0, 1).reshape(partial.shape)
    block_recon = lax.psum_scatter(lat_order, LAT, scatter_dimension=0, tiled=True)
    recon = butterfly_sum(block_recon.astype(jnp.float32), "grp", n_grp, jnp.bfloat16)
    error_own = recon + dec_bias - own_batch.astype(jnp.float32)
    grad_own = (2.0 * error_own).astype(jnp.bfloat16)
    grad_mine = lax.all_gather(grad_own, "chip", axis=0, tiled=True)
    grad_rows = jnp.concatenate([grad_mine, swap_cores(grad_mine)], axis=0)
    grad_active = jnp.dot(grad_rows, weight, preferred_element_type=jnp.float32)
    decoder_grad = lax.dot_general(
        grad_rows, active, (((0,), (0,)), ((), ())), preferred_element_type=jnp.float32
    )
    grad_pre = (grad_active + penalty) * jax.nn.sigmoid(sharpness * preact)
    encoder_grad = lax.dot_general(
        centered,
        grad_pre.astype(jnp.bfloat16),
        (((0,), (0,)), ((), ())),
        preferred_element_type=jnp.float32,
    )
    grad_raw = encoder_grad + decoder_grad
    bias_raw = jnp.sum(grad_pre, axis=0)
    local_squares = jnp.sum(grad_raw * grad_raw) + jnp.sum(bias_raw * bias_raw)
    squares = jnp.broadcast_to(local_squares, (1, 128))
    squares = butterfly_sum(squares, "core", 2, jnp.float32)
    squares = butterfly_sum(squares, "chip", n_chip, jnp.float32)
    total_squares = butterfly_sum(squares, "grp", n_grp, jnp.float32)[0, 0]
    entries = (weight.shape[0] + 1) * weight.shape[1] * 2 * n_chip * n_grp
    factor = jnp.minimum(1.0, 1.0 / jnp.sqrt(total_squares / entries + epsilon))
    return (
        (grad_raw * factor).astype(jnp.bfloat16),
        bias_raw * factor,
        error_own.astype(jnp.bfloat16),
    )


def solution(mesh):
    devices = np.asarray(mesh.devices)
    n_grp, n_lat = devices.shape
    split = Mesh(devices.reshape(n_grp, n_lat // 2, 2), ALL)
    return jax.shard_map(
        body,
        mesh=split,
        in_specs=(P(LAT, None), P(), P(None, ALL), P(ALL), P()),
        out_specs=(P(None, ALL), P(ALL), P(LAT, None)),
        check_vma=False,
    )
```

profile of v0, /device:TPU:2, one launch (start us, length us, event | category | flops | bytes accessed | tf_op | source)
XLA Modules:
  0.0 399.3 jit_solution(17982487750044333137)
XLA Ops:
  8.0 67.5 %all-gather.3.cloned.1.call-done = bf16[128,8192]{1,0:T(8,128)(2,1)} async-done(((bf16[8,8192]{1,0:T(8,128)(2,1)}), bf16[128,8192]{1,0:T(8,128)(2,1)}) %all-gather.3.cloned.1.call-update) | async-done | bytes 2097168 | tf_op jit(solution)/shard_map/all_gather | solution.py:41
  77.4 2.0 gather_fusion
  79.4 2.4 collective-permute-done
  81.8 3.5 convolution_convert_fusion.1
  90.3 3.0 reverse_select_fusion
  93.4 104.6 %reduce-scatter.2.cloned.1.call-done = bf16[8,8192]{1,0:T(8,128)(2,1)} async-done(((bf16[256,8192]{1,0:T(8,128)(2,1)}), bf16[8,8192]{1,0:T(8,128)(2,1)}) %reduce-scatter.2.cloned.1.call-update) | async-done | bytes 131088 | tf_op jit(solution)/shard_map/reduce_scatter | solution.py:67
  198.0 3.5 collective-permute-start.1
  201.5 3.6 collective-permute-done.1
  206.1 4.4 %collective-permute-start.2 = (bf16[8,8192]{1,0:T(8,128)(2,1)S(1)}, bf16[8,8192]{1,0:T(8,128)(2,1)S(1)}, u32[]{:S(2)}, u32[]{:S(2)}) collective-permute-start(bf16[8,8192]{1,0:T(8,128)(2,1)S(1)} %add_convert_fusion.2), channel_id=1, source_target_pairs={{0,64},{32,96},{64,0},{96,32},{128,192},{160,224},{192,128},{224,1... | collective-permute-start | bytes 393224 | tf_op jit(solution)/shard_map/ppermute | solution.py:23
  210.5 4.7 %collective-permute-done.2 = bf16[8,8192]{1,0:T(8,128)(2,1)S(1)} collective-permute-done((bf16[8,8192]{1,0:T(8,128)(2,1)S(1)}, bf16[8,8192]{1,0:T(8,128)(2,1)S(1)}, u32[]{:S(2)}, u32[]{:S(2)}) %collective-permute-start.2) | collective-permute-done | bytes 131104 | tf_op jit(solution)/shard_map/ppermute | solution.py:23
  215.3 8.0 %collective-permute-start.3 = (bf16[8,8192]{1,0:T(8,128)(2,1)S(1)}, bf16[8,8192]{1,0:T(8,128)(2,1)S(1)}, u32[]{:S(2)}, u32[]{:S(2)}) collective-permute-start(bf16[8,8192]{1,0:T(8,128)(2,1)S(1)} %add_convert_fusion.1), channel_id=1, source_target_pairs={{0,128},{32,160},{64,192},{96,224},{128,0},{160,32},{192,64},{224,... | collective-permute-start | bytes 393224 | tf_op jit(solution)/shard_map/ppermute | solution.py:23
  223.3 7.2 %collective-permute-done.3 = bf16[8,8192]{1,0:T(8,128)(2,1)S(1)} collective-permute-done((bf16[8,8192]{1,0:T(8,128)(2,1)S(1)}, bf16[8,8192]{1,0:T(8,128)(2,1)S(1)}, u32[]{:S(2)}, u32[]{:S(2)}) %collective-permute-start.3) | collective-permute-done | bytes 131104 | tf_op jit(solution)/shard_map/ppermute | solution.py:23
  230.5 11.7 %collective-permute-start.4 = (bf16[8,8192]{1,0:T(8,128)(2,1)S(1)}, bf16[8,8192]{1,0:T(8,128)(2,1)S(1)}, u32[]{:S(2)}, u32[]{:S(2)}) collective-permute-start(bf16[8,8192]{1,0:T(8,128)(2,1)S(1)} %add_convert_fusion), channel_id=1, source_target_pairs={{0,256},{32,288},{64,320},{96,352},{128,384},{160,416},{192,448},{... | collective-permute-start | bytes 393224 | tf_op jit(solution)/shard_map/ppermute | solution.py:23
  242.2 6.7 %collective-permute-done.4 = bf16[8,8192]{1,0:T(8,128)(2,1)S(1)} collective-permute-done((bf16[8,8192]{1,0:T(8,128)(2,1)S(1)}, bf16[8,8192]{1,0:T(8,128)(2,1)S(1)}, u32[]{:S(2)}, u32[]{:S(2)}) %collective-permute-start.4) | collective-permute-done | bytes 131104 | tf_op jit(solution)/shard_map/ppermute | solution.py:23
  250.7 58.8 %all-gather.5.cloned.1.call-done = bf16[128,8192]{1,0:T(8,128)(2,1)} async-done(((bf16[8,8192]{1,0:T(8,128)(2,1)}), bf16[128,8192]{1,0:T(8,128)(2,1)}) %all-gather.5.cloned.1.call-update) | async-done | bytes 2097168 | tf_op jit(solution)/shard_map/all_gather | solution.py:71
  313.1 2.6 collective-permute-done.5
  319.6 4.4 %multiply_reduce_fusion = (f32[]{:T(128)}, f32[8192,128]{1,0:T(8,128)}) fusion(f32[8192,128]{1,0:T(8,128)S(1)} %fusion.3, bf16[256,8192]{1,0:T(8,128)(2,1)S(1)} %constant_dynamic-update-slice_fusion, f32[256,128]{1,0:T(8,128)S(1)} %fusion.7), kind=kOutput, calls=%fused_computation.10 | convolution fusion | flops 540278784 | bytes 12713988 | tf_op jit(solution)/shard_map/dot_general | solution.py:74
  325.3 2.0 collective-permute-start.6
  328.3 2.8 collective-permute-start.7
  331.1 2.7 collective-permute-done.7
  333.7 4.0 collective-permute-start.8
  337.7 2.9 collective-permute-done.8
  340.7 2.2 collective-permute-start.9
  342.8 3.3 collective-permute-done.9
  346.1 3.4 collective-permute-start.10
  349.5 3.6 collective-permute-done.10
  353.0 3.5 collective-permute-start.11
  356.5 2.0 collective-permute-done.11
  358.5 4.4 %collective-permute-start.12 = (f32[1,128]{1,0:T(1,128)S(1)}, f32[1,128]{1,0:T(1,128)S(1)}, u32[]{:S(2)}, u32[]{:S(2)}) collective-permute-start(f32[1,128]{1,0:T(1,128)S(1)} %add.281), channel_id=1, source_target_pairs={{0,64},{32,96},{64,0},{96,32},{128,192},{160,224},{192,128},{224,1... | collective-permute-start | bytes 1544 | tf_op jit(solution)/shard_map/ppermute | solution.py:23
  364.8 7.6 %collective-permute-start.13 = (f32[1,128]{1,0:T(1,128)S(1)}, f32[1,128]{1,0:T(1,128)S(1)}, u32[]{:S(2)}, u32[]{:S(2)}) collective-permute-start(f32[1,128]{1,0:T(1,128)S(1)} %add.282), channel_id=1, source_target_pairs={{0,128},{32,160},{64,192},{96,224},{128,0},{160,32},{192,64},{224,... | collective-permute-start | bytes 1544 | tf_op jit(solution)/shard_map/ppermute | solution.py:23
  374.1 12.8 %collective-permute-start.14 = (f32[1,128]{1,0:T(1,128)S(1)}, f32[1,128]{1,0:T(1,128)S(1)}, u32[]{:S(2)}, u32[]{:S(2)}) collective-permute-start(f32[1,128]{1,0:T(1,128)S(1)} %add.283), channel_id=1, source_target_pairs={{0,256},{32,288},{64,320},{96,352},{128,384},{160,416},{192,448},{... | collective-permute-start | bytes 1544 | tf_op jit(solution)/shard_map/ppermute | solution.py:23
  389.0 3.7 multiply_convert_fusion
  (48 shorter events, 24.5 us)
Async XLA Ops:
  7.2 80.1 %copy-start = (bf16[8192,128]{1,0:T(8,128)(2,1)S(1)}, bf16[8192,128]{1,0:T(8,128)(2,1)}, u32[]{:S(2)}) copy-start(bf16[8192,128]{1,0:T(8,128)(2,1)} %param.7) | copy-start | bytes 6291460
  7.2 68.3 %all-gather.3.cloned.1.call-start = ((), (), s32[]{:S(2)}) async-start(), calls=%async_computation.1 | async-start | bytes 2228224 | tf_op jit(solution)/shard_map/all_gather | solution.py:41
  7.9 190.1 %reduce-scatter.2.cloned.1.call-start = ((), (), s32[]{:S(2)}) async-start(), calls=%async_computation.2 | async-start | bytes 4325376 | tf_op jit(solution)/shard_map/reduce_scatter | solution.py:67
  75.4 6.4 %collective-permute-start = (bf16[128,8192]{1,0:T(8,128)(2,1)}, bf16[128,8192]{1,0:T(8,128)(2,1)}, u32[]{:S(2)}, u32[]{:S(2)}) collective-permute-start(bf16[128,8192]{1,0:T(8,128)(2,1)} %all-gather.3.cloned.1.call-done), channel_id=1, source_target_pairs={{0,1},{1,0},{2,3},{3,2},{4,5},{5,4},{6,7},{7,6},{8,9},{9,8},{10,11... | collective-permute-start | bytes 6291464 | tf_op jit(solution)/shard_map/ppermute | solution.py:30
  79.4 7.9 %copy-start.3 = (f32[8192]{0:T(1024)S(1)}, f32[8192]{0:T(1024)}, u32[]{:S(2)}) copy-start(f32[8192]{0:T(1024)} %param.9) | copy-start | bytes 98308
  79.4 7.9 %copy-start.4 = (f32[128]{0:T(128)S(1)}, f32[128]{0:T(128)}, u32[]{:S(2)}) copy-start(f32[128]{0:T(128)} %param.8) | copy-start | bytes 1540
  85.3 1.9 copy-start.1
  93.4 216.1 %all-gather.5.cloned.1.call-start = ((), (), s32[]{:S(2)}) async-start(), calls=%async_computation.3 | async-start | bytes 2228224 | tf_op jit(solution)/shard_map/all_gather | solution.py:71
  198.0 7.1 %collective-permute-start.1 = (bf16[8,8192]{1,0:T(8,128)(2,1)}, bf16[8,8192]{1,0:T(8,128)(2,1)S(1)}, u32[]{:S(2)}, u32[]{:S(2)}) collective-permute-start(bf16[8,8192]{1,0:T(8,128)(2,1)} %reduce-scatter.2.cloned.1.call-done), channel_id=1, source_target_pairs={{0,32},{32,0},{64,96},{96,64},{128,160},{160,128},{192,224},{224,1... | collective-permute-start | bytes 393224 | tf_op jit(solution)/shard_map/ppermute | solution.py:23
  206.1 9.2 %collective-permute-start.2 = (bf16[8,8192]{1,0:T(8,128)(2,1)S(1)}, bf16[8,8192]{1,0:T(8,128)(2,1)S(1)}, u32[]{:S(2)}, u32[]{:S(2)}) collective-permute-start(bf16[8,8192]{1,0:T(8,128)(2,1)S(1)} %add_convert_fusion.2), channel_id=1, source_target_pairs={{0,64},{32,96},{64,0},{96,32},{128,192},{160,224},{192,128},{224,1... | collective-permute-start | bytes 393224 | tf_op jit(solution)/shard_map/ppermute | solution.py:23
  215.3 15.2 %collective-permute-start.3 = (bf16[8,8192]{1,0:T(8,128)(2,1)S(1)}, bf16[8,8192]{1,0:T(8,128)(2,1)S(1)}, u32[]{:S(2)}, u32[]{:S(2)}) collective-permute-start(bf16[8,8192]{1,0:T(8,128)(2,1)S(1)} %add_convert_fusion.1), channel_id=1, source_target_pairs={{0,128},{32,160},{64,192},{96,224},{128,0},{160,32},{192,64},{224,... | collective-permute-start | bytes 393224 | tf_op jit(solution)/shard_map/ppermute | solution.py:23
  230.5 18.4 %collective-permute-start.4 = (bf16[8,8192]{1,0:T(8,128)(2,1)S(1)}, bf16[8,8192]{1,0:T(8,128)(2,1)S(1)}, u32[]{:S(2)}, u32[]{:S(2)}) collective-permute-start(bf16[8,8192]{1,0:T(8,128)(2,1)S(1)} %add_convert_fusion), channel_id=1, source_target_pairs={{0,256},{32,288},{64,320},{96,352},{128,384},{160,416},{192,448},{... | collective-permute-start | bytes 393224 | tf_op jit(solution)/shard_map/ppermute | solution.py:23
  309.5 6.3 %collective-permute-start.5 = (bf16[128,8192]{1,0:T(8,128)(2,1)}, bf16[128,8192]{1,0:T(8,128)(2,1)S(1)}, u32[]{:S(2)}, u32[]{:S(2)}) collective-permute-start(bf16[128,8192]{1,0:T(8,128)(2,1)} %all-gather.5.cloned.1.call-done), channel_id=1, source_target_pairs={{0,1},{1,0},{2,3},{3,2},{4,5},{5,4},{6,7},{7,6},{8,9},{9,8},{10,11... | collective-permute-start | bytes 6291464 | tf_op jit(solution)/shard_map/ppermute | solution.py:30
  315.9 2.2 copy-start.2
  325.3 3.0 collective-permute-start.6
  328.3 5.4 %collective-permute-start.7 = (f32[1,128]{1,0:T(1,128)S(1)}, f32[1,128]{1,0:T(1,128)S(1)}, u32[]{:S(2)}, u32[]{:S(2)}) collective-permute-start(f32[1,128]{1,0:T(1,128)S(1)} %broadcast_add_fusion), channel_id=1, source_target_pairs={{0,2},{2,0},{4,6},{6,4},{8,10},{10,8},{12,14},{14,12},{16,18},{18,... | collective-permute-start | bytes 1544 | tf_op jit(solution)/shard_map/ppermute | solution.py:23
  333.7 6.9 %collective-permute-start.8 = (f32[1,128]{1,0:T(1,128)S(1)}, f32[1,128]{1,0:T(1,128)S(1)}, u32[]{:S(2)}, u32[]{:S(2)}) collective-permute-start(f32[1,128]{1,0:T(1,128)S(1)} %fusion.30), channel_id=1, source_target_pairs={{0,4},{2,6},{4,0},{6,2},{8,12},{10,14},{12,8},{14,10},{16,20},{18,... | collective-permute-start | bytes 1544 | tf_op jit(solution)/shard_map/ppermute | solution.py:23
  340.7 5.4 %collective-permute-start.9 = (f32[1,128]{1,0:T(1,128)S(1)}, f32[1,128]{1,0:T(1,128)S(1)}, u32[]{:S(2)}, u32[]{:S(2)}) collective-permute-start(f32[1,128]{1,0:T(1,128)S(1)} %add.278), channel_id=1, source_target_pairs={{0,8},{2,10},{4,12},{6,14},{8,0},{10,2},{12,4},{14,6},{16,24},{18,... | collective-permute-start | bytes 1544 | tf_op jit(solution)/shard_map/ppermute | solution.py:23
  346.1 6.9 %collective-permute-start.10 = (f32[1,128]{1,0:T(1,128)S(1)}, f32[1,128]{1,0:T(1,128)S(1)}, u32[]{:S(2)}, u32[]{:S(2)}) collective-permute-start(f32[1,128]{1,0:T(1,128)S(1)} %add.279), channel_id=1, source_target_pairs={{0,16},{2,18},{4,20},{6,22},{8,24},{10,26},{12,28},{14,30},{16,0},... | collective-permute-start | bytes 1544 | tf_op jit(solution)/shard_map/ppermute | solution.py:23
  353.0 5.4 %collective-permute-start.11 = (f32[1,128]{1,0:T(1,128)S(1)}, f32[1,128]{1,0:T(1,128)S(1)}, u32[]{:S(2)}, u32[]{:S(2)}) collective-permute-start(f32[1,128]{1,0:T(1,128)S(1)} %add.280), channel_id=1, source_target_pairs={{0,32},{32,0},{64,96},{96,64},{128,160},{160,128},{192,224},{224,1... | collective-permute-start | bytes 1544 | tf_op jit(solution)/shard_map/ppermute | solution.py:23
  358.5 6.3 %collective-permute-start.12 = (f32[1,128]{1,0:T(1,128)S(1)}, f32[1,128]{1,0:T(1,128)S(1)}, u32[]{:S(2)}, u32[]{:S(2)}) collective-permute-start(f32[1,128]{1,0:T(1,128)S(1)} %add.281), channel_id=1, source_target_pairs={{0,64},{32,96},{64,0},{96,32},{128,192},{160,224},{192,128},{224,1... | collective-permute-start | bytes 1544 | tf_op jit(solution)/shard_map/ppermute | solution.py:23
  364.8 9.3 %collective-permute-start.13 = (f32[1,128]{1,0:T(1,128)S(1)}, f32[1,128]{1,0:T(1,128)S(1)}, u32[]{:S(2)}, u32[]{:S(2)}) collective-permute-start(f32[1,128]{1,0:T(1,128)S(1)} %add.282), channel_id=1, source_target_pairs={{0,128},{32,160},{64,192},{96,224},{128,0},{160,32},{192,64},{224,... | collective-permute-start | bytes 1544 | tf_op jit(solution)/shard_map/ppermute | solution.py:23
  374.1 14.3 %collective-permute-start.14 = (f32[1,128]{1,0:T(1,128)S(1)}, f32[1,128]{1,0:T(1,128)S(1)}, u32[]{:S(2)}, u32[]{:S(2)}) collective-permute-start(f32[1,128]{1,0:T(1,128)S(1)} %add.283), channel_id=1, source_target_pairs={{0,256},{32,288},{64,320},{96,352},{128,384},{160,416},{192,448},{... | collective-permute-start | bytes 1544 | tf_op jit(solution)/shard_map/ppermute | solution.py:23
Sparse Core Ops, SparseCore 0:
  11.0 64.3 all-gather.2
  93.5 104.5 reduce-scatter.1
  250.8 58.6 all-gather.4
where the time goes:
time: 400 us; the launch traced here: 399 us
  waiting for transfers between devices  279 us (70%)
  starting transfers between devices  74.1 us (19%)
  between operations  15.4 us (4%)
  matrix products  13.3 us (3%)
  other arithmetic  10.7 us (3%)
  local copies, waits for them, and re-layouts  6.56 us (2%)
    reduce_scatter x1, waiting for transfers between devices, body(): lax.psum_scatter(lat_order, LAT, scatter_dimension=0, tiled=True)  105 us
    ppermute x13, starting transfers between devices, butterfly_sum(): lax.ppermute(sent, axis, xor_pairs(n, bit)).astype(jnp.float32)  70.2 us
    all_gather x1, waiting for transfers between devices, body(): mine = lax.all_gather(stream, 'chip', axis=0, tiled=True)  67.5 us
    all_gather x1, waiting for transfers between devices, body(): grad_mine = lax.all_gather(grad_own, 'chip', axis=0, tiled=True)  58.8 us
    ppermute x13, waiting for transfers between devices, butterfly_sum(): lax.ppermute(sent, axis, xor_pairs(n, bit)).astype(jnp.float32)  42.7 us
  transfers between devices with their start and end apart: 18, of which 18 were waited for; matrix products, arithmetic and copies ran while one was open for 1% of the time, Pallas kernels for 0%

commit v1 on v0

--- a/solution.py
+++ b/solution.py
@@ -68,7 +68,9 @@
     recon = butterfly_sum(block_recon.astype(jnp.float32), "grp", n_grp, jnp.bfloat16)
     error_own = recon + dec_bias - own_batch.astype(jnp.float32)
     grad_own = (2.0 * error_own).astype(jnp.bfloat16)
-    grad_mine = lax.all_gather(grad_own, "chip", axis=0, tiled=True)
+    grad_mine = jnp.concatenate(
+        lax.all_to_all(jnp.stack([grad_own] * lax.psum(1, "chip"), axis=0), "chip", 0, 0), axis=0
+    )
     grad_rows = jnp.concatenate([grad_mine, swap_cores(grad_mine)], axis=0)
     grad_active = jnp.dot(grad_rows, weight, preferred_element_type=jnp.float32)
     decoder_grad = lax.dot_general(

time: 400 us -> 377 us (0.943)
  waiting for transfers between devices: 279 us -> 238 us
  blocking collectives: 0 us -> 36.7 us
  starting transfers between devices: 74.1 us -> 58 us
    all_gather x1 -> x0, waiting for transfers between devices: 58.8 us -> none  [body(): grad_mine = lax.all_gather(grad_own, 'chip', axis=0, tiled=True)]
    all_to_all x0 -> x1, blocking collectives: none -> 36.7 us  [body(): lax.all_to_all(jnp.stack([grad_own] * lax.psum(1, 'chip'), axis=0), 'chip...]
    ppermute x13, starting transfers between devices: 70.2 us -> 53.8 us  [butterfly_sum(): lax.ppermute(sent, axis, xor_pairs(n, bit)).astype(jnp.float32)]
    ppermute x13, waiting for transfers between devices: 42.7 us -> 58.9 us  [butterfly_sum(): lax.ppermute(sent, axis, xor_pairs(n, bit)).astype(jnp.float32)]
  transfers between devices with their start and end apart: 18 -> 17, of which waited for: 18 -> 17; matrix products, arithmetic and copies ran while one was open for 1% -> 1% of each run, Pallas kernels for 0% -> 0%
where the time goes in v1:
time: 377 us
  waiting for transfers between devices  238 us (63%)
  starting transfers between devices  58 us (15%)
  blocking collectives  36.7 us (10%)
  between operations  15.7 us (4%)
  matrix products  12.8 us (3%)
  other arithmetic  10.6 us (3%)
  local copies, waits for them, and re-layouts  4.59 us (1%)
    reduce_scatter x1, waiting for transfers between devices, body(): lax.psum_scatter(lat_order, LAT, scatter_dimension=0, tiled=True)  105 us
    all_gather x1, waiting for transfers between devices, body(): mine = lax.all_gather(stream, 'chip', axis=0, tiled=True)  67.5 us
    ppermute x13, waiting for transfers between devices, butterfly_sum(): lax.ppermute(sent, axis, xor_pairs(n, bit)).astype(jnp.float32)  58.9 us
    ppermute x13, starting transfers between devices, butterfly_sum(): lax.ppermute(sent, axis, xor_pairs(n, bit)).astype(jnp.float32)  53.8 us
    all_to_all x1, blocking collectives, body(): lax.all_to_all(jnp.stack([grad_own] * lax.psum(1, 'chip'), axis=0), 'chip...  36.7 us
  transfers between devices with their start and end apart: 17, of which 17 were waited for; matrix products, arithmetic and copies ran while one was open for 1% of the time, Pallas kernels for 0%

profile of v1, /device:TPU:2, one launch (start us, length us, event | category | flops | bytes accessed | tf_op | source)
XLA Modules:
  0.0 376.6 jit_solution(11228584562278177150)
XLA Ops:
  8.0 67.5 %all-gather.2.cloned.1.call-done = bf16[128,8192]{1,0:T(8,128)(2,1)} async-done(((bf16[8,8192]{1,0:T(8,128)(2,1)}), bf16[128,8192]{1,0:T(8,128)(2,1)}) %all-gather.2.cloned.1.call-update) | async-done | bytes 2097168 | tf_op jit(solution)/shard_map/all_gather | solution.py:41
  77.4 2.0 gather_fusion
  79.4 2.4 collective-permute-done
  81.8 3.5 convolution_convert_fusion.1
  90.3 3.0 reverse_select_fusion
  93.4 104.7 %reduce-scatter.2.cloned.1.call-done = bf16[8,8192]{1,0:T(8,128)(2,1)} async-done(((bf16[256,8192]{1,0:T(8,128)(2,1)}), bf16[8,8192]{1,0:T(8,128)(2,1)}) %reduce-scatter.2.cloned.1.call-update) | async-done | bytes 131088 | tf_op jit(solution)/shard_map/reduce_scatter | solution.py:67
  198.0 3.4 collective-permute-start.1
  201.5 3.6 collective-permute-done.1
  206.0 4.4 %collective-permute-start.2 = (bf16[8,8192]{1,0:T(8,128)(2,1)S(1)}, bf16[8,8192]{1,0:T(8,128)(2,1)S(1)}, u32[]{:S(2)}, u32[]{:S(2)}) collective-permute-start(bf16[8,8192]{1,0:T(8,128)(2,1)S(1)} %add_convert_fusion.2), channel_id=1, source_target_pairs={{0,64},{32,96},{64,0},{96,32},{128,192},{160,224},{192,128},{224,1... | collective-permute-start | bytes 393224 | tf_op jit(solution)/shard_map/ppermute | solution.py:23
  210.5 4.7 %collective-permute-done.2 = bf16[8,8192]{1,0:T(8,128)(2,1)S(1)} collective-permute-done((bf16[8,8192]{1,0:T(8,128)(2,1)S(1)}, bf16[8,8192]{1,0:T(8,128)(2,1)S(1)}, u32[]{:S(2)}, u32[]{:S(2)}) %collective-permute-start.2) | collective-permute-done | bytes 131104 | tf_op jit(solution)/shard_map/ppermute | solution.py:23
  215.2 8.0 %collective-permute-start.3 = (bf16[8,8192]{1,0:T(8,128)(2,1)S(1)}, bf16[8,8192]{1,0:T(8,128)(2,1)S(1)}, u32[]{:S(2)}, u32[]{:S(2)}) collective-permute-start(bf16[8,8192]{1,0:T(8,128)(2,1)S(1)} %add_convert_fusion.1), channel_id=1, source_target_pairs={{0,128},{32,160},{64,192},{96,224},{128,0},{160,32},{192,64},{224,... | collective-permute-start | bytes 393224 | tf_op jit(solution)/shard_map/ppermute | solution.py:23
  223.2 7.2 %collective-permute-done.3 = bf16[8,8192]{1,0:T(8,128)(2,1)S(1)} collective-permute-done((bf16[8,8192]{1,0:T(8,128)(2,1)S(1)}, bf16[8,8192]{1,0:T(8,128)(2,1)S(1)}, u32[]{:S(2)}, u32[]{:S(2)}) %collective-permute-start.3) | collective-permute-done | bytes 131104 | tf_op jit(solution)/shard_map/ppermute | solution.py:23
  230.5 11.7 %collective-permute-start.4 = (bf16[8,8192]{1,0:T(8,128)(2,1)S(1)}, bf16[8,8192]{1,0:T(8,128)(2,1)S(1)}, u32[]{:S(2)}, u32[]{:S(2)}) collective-permute-start(bf16[8,8192]{1,0:T(8,128)(2,1)S(1)} %add_convert_fusion), channel_id=1, source_target_pairs={{0,256},{32,288},{64,320},{96,352},{128,384},{160,416},{192,448},{... | collective-permute-start | bytes 393224 | tf_op jit(solution)/shard_map/ppermute | solution.py:23
  242.2 6.7 %collective-permute-done.4 = bf16[8,8192]{1,0:T(8,128)(2,1)S(1)} collective-permute-done((bf16[8,8192]{1,0:T(8,128)(2,1)S(1)}, bf16[8,8192]{1,0:T(8,128)(2,1)S(1)}, u32[]{:S(2)}, u32[]{:S(2)}) %collective-permute-start.4) | collective-permute-done | bytes 131104 | tf_op jit(solution)/shard_map/ppermute | solution.py:23
  250.8 36.7 %all_to_all.5 = bf16[16,8,8192]{2,1,0:T(8,128)(2,1)S(1)} all-to-all(bf16[16,8,8192]{2,1,0:T(8,128)(2,1)S(1)} %stack.2), channel_id=1, replica_groups=mesh['grp'=16,'chip'=16,'core'=2] {'chip'}, dimensions={0} | all-to-all | bytes 4194304 | tf_op jit(solution)/shard_map/all_to_all | solution.py:72
  287.5 2.2 collective-permute-start.5
  289.7 4.1 %collective-permute-done.5 = bf16[128,8192]{1,0:T(8,128)(2,1)S(1)} collective-permute-done((bf16[128,8192]{1,0:T(8,128)(2,1)S(1)}, bf16[128,8192]{1,0:T(8,128)(2,1)S(1)}, u32[]{:S(2)}, u32[]{:S(2)}) %collective-permute-start.5) | collective-permute-done | bytes 2097184 | tf_op jit(solution)/shard_map/ppermute | solution.py:30
  297.2 3.9 %multiply_reduce_fusion = (f32[]{:T(128)}, f32[8192,128]{1,0:T(8,128)}) fusion(f32[8192,128]{1,0:T(8,128)S(1)} %fusion.3, f32[256,128]{1,0:T(8,128)S(1)} %fusion.9, bf16[128,8192]{1,0:T(8,128)(2,1)S(1)} %collective-permute-done.5, bf16[128,8192]{1,0:T(8,128)(2,1)S(1)} %bitcast.16), kind=kOutput, calls=%fused_computation.11 | convolution fusion | flops 548667392 | bytes 12713988 | tf_op jit(solution)/shard_map/dot_general | solution.py:76
  302.4 2.0 collective-permute-start.6
  305.4 3.4 collective-permute-start.7
  308.8 2.1 collective-permute-done.7
  310.9 2.7 collective-permute-start.8
  313.6 4.2 %collective-permute-done.8 = f32[1,128]{1,0:T(1,128)S(1)} collective-permute-done((f32[1,128]{1,0:T(1,128)S(1)}, f32[1,128]{1,0:T(1,128)S(1)}, u32[]{:S(2)}, u32[]{:S(2)}) %collective-permute-start.8) | collective-permute-done | bytes 544 | tf_op jit(solution)/shard_map/ppermute | solution.py:23
  319.7 3.5 collective-permute-done.9
  323.2 2.7 collective-permute-start.10
  326.0 4.2 %collective-permute-done.10 = f32[1,128]{1,0:T(1,128)S(1)} collective-permute-done((f32[1,128]{1,0:T(1,128)S(1)}, f32[1,128]{1,0:T(1,128)S(1)}, u32[]{:S(2)}, u32[]{:S(2)}) %collective-permute-start.10) | collective-permute-done | bytes 544 | tf_op jit(solution)/shard_map/ppermute | solution.py:23
  332.1 3.5 collective-permute-done.11
  337.5 4.4 %collective-permute-done.12 = f32[1,128]{1,0:T(1,128)S(1)} collective-permute-done((f32[1,128]{1,0:T(1,128)S(1)}, f32[1,128]{1,0:T(1,128)S(1)}, u32[]{:S(2)}, u32[]{:S(2)}) %collective-permute-start.12) | collective-permute-done | bytes 544 | tf_op jit(solution)/shard_map/ppermute | solution.py:23
  343.9 7.4 %collective-permute-done.13 = f32[1,128]{1,0:T(1,128)S(1)} collective-permute-done((f32[1,128]{1,0:T(1,128)S(1)}, f32[1,128]{1,0:T(1,128)S(1)}, u32[]{:S(2)}, u32[]{:S(2)}) %collective-permute-start.13) | collective-permute-done | bytes 544 | tf_op jit(solution)/shard_map/ppermute | solution.py:23
  351.3 7.8 %collective-permute-start.14 = (f32[1,128]{1,0:T(1,128)S(1)}, f32[1,128]{1,0:T(1,128)S(1)}, u32[]{:S(2)}, u32[]{:S(2)}) collective-permute-start(f32[1,128]{1,0:T(1,128)S(1)} %add.283), channel_id=1, source_target_pairs={{0,256},{32,288},{64,320},{96,352},{128,384},{160,416},{192,448},{... | collective-permute-start | bytes 1544 | tf_op jit(solution)/shard_map/ppermute | solution.py:23
  359.0 6.4 %collective-permute-done.14 = f32[1,128]{1,0:T(1,128)S(1)} collective-permute-done((f32[1,128]{1,0:T(1,128)S(1)}, f32[1,128]{1,0:T(1,128)S(1)}, u32[]{:S(2)}, u32[]{:S(2)}) %collective-permute-start.14) | collective-permute-done | bytes 544 | tf_op jit(solution)/shard_map/ppermute | solution.py:23
  366.0 3.7 multiply_convert_fusion
  (45 shorter events, 23.1 us)
Async XLA Ops:
  7.2 80.1 %copy-start = (bf16[8192,128]{1,0:T(8,128)(2,1)S(1)}, bf16[8192,128]{1,0:T(8,128)(2,1)}, u32[]{:S(2)}) copy-start(bf16[8192,128]{1,0:T(8,128)(2,1)} %param.7) | copy-start | bytes 6291460
  7.2 68.3 %all-gather.2.cloned.1.call-start = ((), (), s32[]{:S(2)}) async-start(), calls=%async_computation.2 | async-start | bytes 2228224 | tf_op jit(solution)/shard_map/all_gather | solution.py:41
  7.9 190.1 %reduce-scatter.2.cloned.1.call-start = ((), (), s32[]{:S(2)}) async-start(), calls=%async_computation.3 | async-start | bytes 4325376 | tf_op jit(solution)/shard_map/reduce_scatter | solution.py:67
  75.4 6.4 %collective-permute-start = (bf16[128,8192]{1,0:T(8,128)(2,1)}, bf16[128,8192]{1,0:T(8,128)(2,1)}, u32[]{:S(2)}, u32[]{:S(2)}) collective-permute-start(bf16[128,8192]{1,0:T(8,128)(2,1)} %all-gather.2.cloned.1.call-done), channel_id=1, source_target_pairs={{0,1},{1,0},{2,3},{3,2},{4,5},{5,4},{6,7},{7,6},{8,9},{9,8},{10,11... | collective-permute-start | bytes 6291464 | tf_op jit(solution)/shard_map/ppermute | solution.py:30
  79.4 7.9 %copy-start.3 = (f32[8192]{0:T(1024)S(1)}, f32[8192]{0:T(1024)}, u32[]{:S(2)}) copy-start(f32[8192]{0:T(1024)} %param.9) | copy-start | bytes 98308
  79.4 7.9 %copy-start.4 = (f32[128]{0:T(128)S(1)}, f32[128]{0:T(128)}, u32[]{:S(2)}) copy-start(f32[128]{0:T(128)} %param.8) | copy-start | bytes 1540
  85.3 2.0 copy-start.1
  198.0 7.1 %collective-permute-start.1 = (bf16[8,8192]{1,0:T(8,128)(2,1)}, bf16[8,8192]{1,0:T(8,128)(2,1)S(1)}, u32[]{:S(2)}, u32[]{:S(2)}) collective-permute-start(bf16[8,8192]{1,0:T(8,128)(2,1)} %reduce-scatter.2.cloned.1.call-done), channel_id=1, source_target_pairs={{0,32},{32,0},{64,96},{96,64},{128,160},{160,128},{192,224},{224,1... | collective-permute-start | bytes 393224 | tf_op jit(solution)/shard_map/ppermute | solution.py:23
  206.0 9.2 %collective-permute-start.2 = (bf16[8,8192]{1,0:T(8,128)(2,1)S(1)}, bf16[8,8192]{1,0:T(8,128)(2,1)S(1)}, u32[]{:S(2)}, u32[]{:S(2)}) collective-permute-start(bf16[8,8192]{1,0:T(8,128)(2,1)S(1)} %add_convert_fusion.2), channel_id=1, source_target_pairs={{0,64},{32,96},{64,0},{96,32},{128,192},{160,224},{192,128},{224,1... | collective-permute-start | bytes 393224 | tf_op jit(solution)/shard_map/ppermute | solution.py:23
  215.2 15.2 %collective-permute-start.3 = (bf16[8,8192]{1,0:T(8,128)(2,1)S(1)}, bf16[8,8192]{1,0:T(8,128)(2,1)S(1)}, u32[]{:S(2)}, u32[]{:S(2)}) collective-permute-start(bf16[8,8192]{1,0:T(8,128)(2,1)S(1)} %add_convert_fusion.1), channel_id=1, source_target_pairs={{0,128},{32,160},{64,192},{96,224},{128,0},{160,32},{192,64},{224,... | collective-permute-start | bytes 393224 | tf_op jit(solution)/shard_map/ppermute | solution.py:23
  230.5 18.4 %collective-permute-start.4 = (bf16[8,8192]{1,0:T(8,128)(2,1)S(1)}, bf16[8,8192]{1,0:T(8,128)(2,1)S(1)}, u32[]{:S(2)}, u32[]{:S(2)}) collective-permute-start(bf16[8,8192]{1,0:T(8,128)(2,1)S(1)} %add_convert_fusion), channel_id=1, source_target_pairs={{0,256},{32,288},{64,320},{96,352},{128,384},{160,416},{192,448},{... | collective-permute-start | bytes 393224 | tf_op jit(solution)/shard_map/ppermute | solution.py:23
  287.5 7.6 %copy-start.2 = (bf16[256,8192]{1,0:T(8,128)(2,1)S(1)}, bf16[256,8192]{1,0:T(8,128)(2,1)}, u32[]{:S(2)}) copy-start(bf16[256,8192]{1,0:T(8,128)(2,1)} %copy-done.1) | copy-start | bytes 12582916
  287.5 6.3 %collective-permute-start.5 = (bf16[128,8192]{1,0:T(8,128)(2,1)S(1)}, bf16[128,8192]{1,0:T(8,128)(2,1)S(1)}, u32[]{:S(2)}, u32[]{:S(2)}) collective-permute-start(bf16[128,8192]{1,0:T(8,128)(2,1)S(1)} %bitcast.14), channel_id=1, source_target_pairs={{0,1},{1,0},{2,3},{3,2},{4,5},{5,4},{6,7},{7,6},{8,9},{9,8},{10,11... | collective-permute-start | bytes 6291464 | tf_op jit(solution)/shard_map/ppermute | solution.py:30
  302.4 3.0 collective-permute-start.6
  305.4 5.4 %collective-permute-start.7 = (f32[1,128]{1,0:T(1,128)S(1)}, f32[1,128]{1,0:T(1,128)S(1)}, u32[]{:S(2)}, u32[]{:S(2)}) collective-permute-start(f32[1,128]{1,0:T(1,128)S(1)} %broadcast_add_fusion), channel_id=1, source_target_pairs={{0,2},{2,0},{4,6},{6,4},{8,10},{10,8},{12,14},{14,12},{16,18},{18,... | collective-permute-start | bytes 1544 | tf_op jit(solution)/shard_map/ppermute | solution.py:23
  310.9 6.9 %collective-permute-start.8 = (f32[1,128]{1,0:T(1,128)S(1)}, f32[1,128]{1,0:T(1,128)S(1)}, u32[]{:S(2)}, u32[]{:S(2)}) collective-permute-start(f32[1,128]{1,0:T(1,128)S(1)} %fusion.32), channel_id=1, source_target_pairs={{0,4},{2,6},{4,0},{6,2},{8,12},{10,14},{12,8},{14,10},{16,20},{18,... | collective-permute-start | bytes 1544 | tf_op jit(solution)/shard_map/ppermute | solution.py:23
  317.8 5.4 %collective-permute-start.9 = (f32[1,128]{1,0:T(1,128)S(1)}, f32[1,128]{1,0:T(1,128)S(1)}, u32[]{:S(2)}, u32[]{:S(2)}) collective-permute-start(f32[1,128]{1,0:T(1,128)S(1)} %add.278), channel_id=1, source_target_pairs={{0,8},{2,10},{4,12},{6,14},{8,0},{10,2},{12,4},{14,6},{16,24},{18,... | collective-permute-start | bytes 1544 | tf_op jit(solution)/shard_map/ppermute | solution.py:23
  323.2 6.9 %collective-permute-start.10 = (f32[1,128]{1,0:T(1,128)S(1)}, f32[1,128]{1,0:T(1,128)S(1)}, u32[]{:S(2)}, u32[]{:S(2)}) collective-permute-start(f32[1,128]{1,0:T(1,128)S(1)} %add.279), channel_id=1, source_target_pairs={{0,16},{2,18},{4,20},{6,22},{8,24},{10,26},{12,28},{14,30},{16,0},... | collective-permute-start | bytes 1544 | tf_op jit(solution)/shard_map/ppermute | solution.py:23
  330.2 5.4 %collective-permute-start.11 = (f32[1,128]{1,0:T(1,128)S(1)}, f32[1,128]{1,0:T(1,128)S(1)}, u32[]{:S(2)}, u32[]{:S(2)}) collective-permute-start(f32[1,128]{1,0:T(1,128)S(1)} %add.280), channel_id=1, source_target_pairs={{0,32},{32,0},{64,96},{96,64},{128,160},{160,128},{192,224},{224,1... | collective-permute-start | bytes 1544 | tf_op jit(solution)/shard_map/ppermute | solution.py:23
  335.6 6.3 %collective-permute-start.12 = (f32[1,128]{1,0:T(1,128)S(1)}, f32[1,128]{1,0:T(1,128)S(1)}, u32[]{:S(2)}, u32[]{:S(2)}) collective-permute-start(f32[1,128]{1,0:T(1,128)S(1)} %add.281), channel_id=1, source_target_pairs={{0,64},{32,96},{64,0},{96,32},{128,192},{160,224},{192,128},{224,1... | collective-permute-start | bytes 1544 | tf_op jit(solution)/shard_map/ppermute | solution.py:23
  341.9 9.3 %collective-permute-start.13 = (f32[1,128]{1,0:T(1,128)S(1)}, f32[1,128]{1,0:T(1,128)S(1)}, u32[]{:S(2)}, u32[]{:S(2)}) collective-permute-start(f32[1,128]{1,0:T(1,128)S(1)} %add.282), channel_id=1, source_target_pairs={{0,128},{32,160},{64,192},{96,224},{128,0},{160,32},{192,64},{224,... | collective-permute-start | bytes 1544 | tf_op jit(solution)/shard_map/ppermute | solution.py:23
  351.3 14.1 %collective-permute-start.14 = (f32[1,128]{1,0:T(1,128)S(1)}, f32[1,128]{1,0:T(1,128)S(1)}, u32[]{:S(2)}, u32[]{:S(2)}) collective-permute-start(f32[1,128]{1,0:T(1,128)S(1)} %add.283), channel_id=1, source_target_pairs={{0,256},{32,288},{64,320},{96,352},{128,384},{160,416},{192,448},{... | collective-permute-start | bytes 1544 | tf_op jit(solution)/shard_map/ppermute | solution.py:23
Sparse Core Ops, SparseCore 0:
  11.0 64.3 all-gather.1
  93.5 104.5 reduce-scatter.1
